TPU v7x, 32 devices: a whole 2x2x4 slice. The times are simulated.
32 devices in a mesh: row: 4 (over z), col: 4 (over y, core), pix: 2 (over x).
Axes of the slice: x: 2, y: 2, z: 4, core: 2. Of those that a mesh axis runs over, the one named last changes fastest.
Arguments:
- sample_frames: bfloat16 [4096, 16384], P(('row', 'col'), 'pix'), may hold values from 0.14 to 26
- reference_frames: bfloat16 [4096, 16384], P(('row', 'col'), 'pix'), may hold values from 0.14 to 26
- gain: float32 [16384], P('pix'), may hold values from 0.5 to 2
- flat: float32 [16384], P('pix'), may hold values from 0.6 to 1.6
- qbin: int32 [16384], P('pix'), may hold values from 0 to 31
- region: int32 [16384], P('pix'), may hold values 0 or 1
- live: int32 [16384], P('pix'), may hold values 0 or 1
Outputs:
- twotime: float32 [4096, 4, 4, 256], P('row', None, 'col', 'pix')
All inputs are finite; a program needn't handle non-finite values. No bound on the sum of `region` or of `live` on one device may be relied on, other than what follows from the above.
Results may differ from a plain program's by a relative error of at most 0.0039.
Values may be sent and summed in bfloat16 or wider, within the bound.
No kernel may reach another device: no remote copies, remote signals or barrier semaphores. Data moves between devices by JAX's collectives and lax.ppermute only.
A program may use at most 128 MiB of HBM per device.

v0:
```python
import math
import jax
import jax.numpy as jnp
from jax import lax
from jax.sharding import PartitionSpec as P

QBINS = 32


def on_device(sample_frames, reference_frames, gain, flat, qbin, region, live):
    block = sample_frames.shape[0]
    factor = gain / flat
    select = (qbin[None, :] == jnp.arange(QBINS, dtype=jnp.int32)[:, None]).astype(jnp.float32)
    ref_select = select * (live * (1 - region)).astype(jnp.float32)[None, :]
    sample_weight = (live * region).astype(jnp.float32)
    corrected_sample = sample_frames.astype(jnp.float32) * factor
    corrected_reference = reference_frames.astype(jnp.float32) * factor
    sums_sample = jnp.dot(corrected_sample, ref_select.T, precision=lax.Precision.HIGHEST)
    sums_reference = jnp.dot(corrected_reference, ref_select.T, precision=lax.Precision.HIGHEST)
    counts = jnp.sum(ref_select, axis=1)
    sums_sample, sums_reference, counts = lax.psum((sums_sample, sums_reference, counts), "pix")
    mean_sample = (sums_sample + 1.0) / (counts + 1.0)
    mean_reference = (sums_reference + 1.0) / (counts + 1.0)
    spread_sample = jnp.dot(mean_sample, select, precision=lax.Precision.HIGHEST)
    spread_reference = jnp.dot(mean_reference, select, precision=lax.Precision.HIGHEST)
    delta_sample = ((corrected_sample / spread_sample - 1.0) * sample_weight).astype(jnp.bfloat16)
    delta_reference = (corrected_reference / spread_reference - 1.0).astype(jnp.bfloat16)
    sample_rows = lax.all_gather(delta_sample, "col", axis=0, tiled=True)
    partial_value = lax.dot_general(
        sample_rows,
        lax.all_gather(delta_reference, "row", axis=0, tiled=True),
        (((1,), (1,)), ((), ())),
        preferred_element_type=jnp.float32,
    )
    groups = lax.axis_size("row")
    scale = 1.0 / math.sqrt(gain.shape[0] * lax.axis_size("pix"))
    partial_value = (partial_value * scale).reshape(sample_rows.shape[0], groups, block)
    whole = lax.psum(partial_value, "pix")
    width = block // lax.axis_size("pix")
    mine = lax.dynamic_slice_in_dim(whole, lax.axis_index("pix") * width, width, 2)
    return mine[:, :, None, :]


def solution(mesh):
    return jax.shard_map(
        on_device,
        mesh=mesh,
        in_specs=(
            P(("row", "col"), "pix"),
            P(("row", "col"), "pix"),
            P("pix"),
            P("pix"),
            P("pix"),
            P("pix"),
            P("pix"),
        ),
        out_specs=P("row", None, "col", "pix"),
        check_vma=False,
    )
```

profile of v0, /device:TPU:0, one launch (start us, length us, event | category | flops | bytes accessed | tf_op | source)
XLA Modules:
  0.0 598.4 jit_solution(18286605986021742596)
XLA Ops:
  6.5 0.0 copy-start
  6.5 0.0 all-reduce.6.cloned.1.call-start
  6.5 0.8 multiply_convert_fusion.1
  7.3 0.8 div.23
  8.1 1.5 select_reduce_fusion
  9.6 9.2 %fusion.5 = f32[256,32]{1,0:T(8,128)} fusion(bf16[256,8192]{1,0:T(8,128)(2,1)} %param.8, f32[8192]{0:T(1024)S(1)} %div.23, f32[8192]{0:T(1024)S(1)} %get-tuple-element.8, s32[8192]{0:T(1024)} %param.11), kind=kOutput, calls=%fused_computation.8 | convolution fusion | flops 810024960 | bytes 4325376 | tf_op jit(solution)/shard_map/dot_general | solution.py:19
  18.8 9.2 %fusion.6 = f32[256,32]{1,0:T(8,128)} fusion(bf16[256,8192]{1,0:T(8,128)(2,1)} %param.7, f32[8192]{0:T(1024)S(1)} %div.23, f32[8192]{0:T(1024)S(1)} %get-tuple-element.8, s32[8192]{0:T(1024)} %param.11), kind=kOutput, calls=%fused_computation.10 | convolution fusion | flops 810024960 | bytes 4325376 | tf_op jit(solution)/shard_map/dot_general | solution.py:18
  28.0 0.0 all-reduce.6.cloned.1.call-update
  28.1 0.0 all-gather.3.cloned.1.call-start
  28.1 26.4 %all-reduce.6.cloned.1.call-done = (f32[256,32]{1,0:T(8,128)}, f32[32]{0:T(128)}, f32[256,32]{1,0:T(8,128)}) async-done(((f32[256,32]{1,0:T(8,128)}, f32[32]{0:T(128)}, f32[256,32]{1,0:T(8,128)}), (f32[256,32]{1,0:T(8,128)}, f32[32]{0:T(128)}, f32[256,32]{1,0:T(8,128)})) %all-reduce.6.cloned.1.call-update) | async-done | bytes 65680 | tf_op jit(solution)/shard_map/psum | solution.py:21
  54.5 0.6 broadcast_add_fusion
  55.1 0.0 copy-done
  55.1 0.0 copy-start.1
  55.1 7.9 %fusion.4 = bf16[256,8192]{1,0:T(8,128)(2,1)} fusion(bf16[256,8192]{1,0:T(8,128)(2,1)} %param.7, f32[8192]{0:T(1024)S(1)} %get-tuple-element.9, f32[8192]{0:T(1024)S(1)} %div.23, s32[8192]{0:T(1024)S(1)} %copy-done, f32[256,32]{1,0:T(8,128)} %get-tuple-element.5, f32[32]{0:T(128)S(1)} %broadcast_add_fusion), kind=kOutput, calls=%fused_computation.6 | convolution fusion | flops 818167808 | bytes 8519808 | tf_op jit(solution)/shard_map/dot_general | solution.py:24
  63.0 0.0 all-gather.3.cloned.1.call-update
  63.0 0.2 all-gather.5.cloned.1.call-start
  63.3 0.0 copy-done.1
  63.3 7.6 %fusion.1 = bf16[256,8192]{1,0:T(8,128)(2,1)} fusion(bf16[256,8192]{1,0:T(8,128)(2,1)} %param.8, f32[8192]{0:T(1024)S(1)} %div.23, s32[8192]{0:T(1024)S(1)} %copy-done, f32[256,32]{1,0:T(8,128)S(1)} %copy-done.1, f32[32]{0:T(128)S(1)} %broadcast_add_fusion), kind=kOutput, calls=%fused_computation.2 | convolution fusion | flops 816070656 | bytes 8487040 | tf_op jit(solution)/shard_map/dot_general | solution.py:25
  70.9 0.0 all-gather.5.cloned.1.call-update
  70.9 0.0 all-reduce.4.cloned.1.call-start
  70.9 98.4 %all-gather.3.cloned.1.call-done = bf16[1024,8192]{1,0:T(8,128)(2,1)} async-done(((bf16[256,8192]{1,0:T(8,128)(2,1)}), bf16[1024,8192]{1,0:T(8,128)(2,1)}) %all-gather.3.cloned.1.call-update) | async-done | bytes 16777232 | tf_op jit(solution)/shard_map/all_gather | solution.py:28
  169.3 288.5 %all-gather.5.cloned.1.call-done = bf16[1024,8192]{1,0:T(8,128)(2,1)} async-done(((bf16[256,8192]{1,0:T(8,128)(2,1)}), bf16[1024,8192]{1,0:T(8,128)(2,1)}) %all-gather.5.cloned.1.call-update) | async-done | bytes 16777232 | tf_op jit(solution)/shard_map/all_gather | solution.py:31
  457.8 24.3 %convolution_multiply_fusion = f32[1024,1024]{0,1:T(8,128)} fusion(bf16[1024,8192]{1,0:T(8,128)(2,1)} %all-gather.3.cloned.1.call-done, bf16[1024,8192]{1,0:T(8,128)(2,1)} %all-gather.5.cloned.1.call-done), kind=kOutput, calls=%fused_computation.13 | convolution fusion | flops 17180917760 | bytes 37748736 | tf_op jit(solution)/shard_map/dot_general | solution.py:29
  482.1 0.0 all-reduce.4.cloned.1.call-update
  482.1 106.2 %all-reduce.4.cloned.1.call-done = f32[1024,4,256]{0,2,1:T(8,128)} async-done(((f32[1024,4,256]{0,2,1:T(8,128)}), f32[1024,4,256]{0,2,1:T(8,128)}) %all-reduce.4.cloned.1.call-update) | async-done | bytes 4194320 | tf_op jit(solution)/shard_map/psum | solution.py:38
  588.3 1.7 constant_dynamic-slice_fusion
  590.1 1.8 copy.9
Async XLA Ops:
  6.5 48.6 %copy-start = (s32[8192]{0:T(1024)S(1)}, s32[8192]{0:T(1024)}, u32[]{:S(2)}) copy-start(s32[8192]{0:T(1024)} %param.11) | copy-start | bytes 98308
  6.5 48.0 %all-reduce.6.cloned.1.call-start = ((), (), s32[]{:S(2)}) async-start(), calls=%async_computation.3 | async-start | bytes 525312 | tf_op jit(solution)/shard_map/psum | solution.py:21
  28.1 141.3 %all-gather.3.cloned.1.call-start = ((), (), s32[]{:S(2)}) async-start(), calls=%async_computation | async-start | bytes 20971520 | tf_op jit(solution)/shard_map/all_gather | solution.py:28
  55.1 8.2 %copy-start.1 = (f32[256,32]{1,0:T(8,128)S(1)}, f32[256,32]{1,0:T(8,128)}, u32[]{:S(2)}) copy-start(f32[256,32]{1,0:T(8,128)} %get-tuple-element.7) | copy-start | bytes 98308
  63.0 394.8 %all-gather.5.cloned.1.call-start = ((), (), s32[]{:S(2)}) async-start(), calls=%async_computation.1 | async-start | bytes 20971520 | tf_op jit(solution)/shard_map/all_gather | solution.py:31
  70.9 517.4 %all-reduce.4.cloned.1.call-start = ((), (), s32[]{:S(2)}) async-start(), calls=%async_computation.2 | async-start | bytes 8388608 | tf_op jit(solution)/shard_map/psum | solution.py:38
Sparse Core Ops, SparseCore 0:
  28.2 26.2 all-reduce.5
  63.2 106.1 all-gather.2
  171.0 286.7 all-gather.4
  482.3 106.0 all-reduce.3
where the time goes:
time: 599 us; the launch traced here: 598 us
  waiting for transfers between devices  519 us (87%)
  matrix products  58.3 us (10%)
  between operations  13.2 us (2%)
    all_gather x1, waiting for transfers between devices, on_device(): lax.all_gather(delta_reference, 'row', axis=0, tiled=True)  288 us
    psum x1, waiting for transfers between devices, on_device(): whole = lax.psum(partial_value, 'pix')  106 us
    all_gather x1, waiting for transfers between devices, on_device(): sample_rows = lax.all_gather(delta_sample, 'col', axis=0, tiled=True)  98.4 us
    psum x1, waiting for transfers between devices, on_device(): lax.psum((sums_sample, sums_reference, counts), 'pix')  26.4 us
    dot_general x1, matrix products, on_device(): lax.dot_general(sample_rows, lax.all_gather(delta_reference, 'row', axis=...  24.3 us
  transfers between devices with their start and end apart: 4, of which 4 were waited for; matrix products, arithmetic and copies ran while one was open for 1% of the time, Pallas kernels for 0%

commit v1 on v0

--- a/solution.py
+++ b/solution.py
@@ -5,6 +5,23 @@
 from jax.sharding import PartitionSpec as P
 
 QBINS = 32
+
+
+def joined_along(pieces, dim):
+    dims = list(pieces.shape[1:])
+    dims[dim] *= pieces.shape[0]
+    return jnp.moveaxis(pieces, 0, dim).reshape(dims)
+
+
+def doubled(value, axis):
+    size, index = (lax.axis_size(axis), lax.axis_index(axis))
+    parts, bit = (value[None], 1)
+    while bit < size:
+        other = lax.ppermute(parts, axis, [(i, i ^ bit) for i in range(size)])
+        low = index & bit == 0
+        parts = jnp.concatenate([jnp.where(low, parts, other), jnp.where(low, other, parts)])
+        bit *= 2
+    return parts
 
 
 def on_device(sample_frames, reference_frames, gain, flat, qbin, region, live):
@@ -25,7 +42,7 @@
     spread_reference = jnp.dot(mean_reference, select, precision=lax.Precision.HIGHEST)
     delta_sample = ((corrected_sample / spread_sample - 1.0) * sample_weight).astype(jnp.bfloat16)
     delta_reference = (corrected_reference / spread_reference - 1.0).astype(jnp.bfloat16)
-    sample_rows = lax.all_gather(delta_sample, "col", axis=0, tiled=True)
+    sample_rows = joined_along(doubled(delta_sample, "col"), 0)
     partial_value = lax.dot_general(
         sample_rows,
         lax.all_gather(delta_reference, "row", axis=0, tiled=True),

time: 599 us -> 491 us (0.82)
  waiting for transfers between devices: 519 us -> 383 us
  other arithmetic: 3.66 us -> 30.8 us
    all_gather x1, waiting for transfers between devices: 288 us -> 61.7 us  [on_device(): lax.all_gather(delta_reference, 'row', axis=0, tiled=True)]
    ppermute x0 -> x2, waiting for transfers between devices: none -> 189 us  [doubled(): other = lax.ppermute(parts, axis, [(i, i ^ bit) for i in range(size)])]
    all_gather x1 -> x0, waiting for transfers between devices: 98.4 us -> none  [on_device(): sample_rows = lax.all_gather(delta_sample, 'col', axis=0, tiled=True)]
    concatenate x0 -> x2, other arithmetic: none -> 14.3 us  [doubled(): jnp.concatenate([jnp.where(low, parts, other), jnp.where(low, other, part...]
    select_n x0 -> x2, other arithmetic: none -> 12.7 us  [doubled(): jnp.where(low, parts, other)]
  transfers between devices with their start and end apart: 4 -> 5, of which waited for: 4 -> 5; matrix products, arithmetic and copies ran while one was open for 1% -> 7% of each run, Pallas kernels for 0% -> 0%
where the time goes in v1:
time: 491 us
  waiting for transfers between devices  383 us (78%)
  matrix products  58.3 us (12%)
  other arithmetic  30.8 us (6%)
  between operations  13.1 us (3%)
    ppermute x2, waiting for transfers between devices, doubled(): other = lax.ppermute(parts, axis, [(i, i ^ bit) for i in range(size)])  189 us
    psum x1, waiting for transfers between devices, on_device(): whole = lax.psum(partial_value, 'pix')  106 us
    all_gather x1, waiting for transfers between devices, on_device(): lax.all_gather(delta_reference, 'row', axis=0, tiled=True)  61.7 us
    psum x1, waiting for transfers between devices, on_device(): lax.psum((sums_sample, sums_reference, counts), 'pix')  26.4 us
    dot_general x1, matrix products, on_device(): lax.dot_general(sample_rows, lax.all_gather(delta_reference, 'row', axis=...  24.3 us
    concatenate x2, other arithmetic, doubled(): jnp.concatenate([jnp.where(low, parts, other), jnp.where(low, other, part...  14.3 us
    select_n x2, other arithmetic, doubled(): jnp.where(low, parts, other)  12.7 us
  transfers between devices with their start and end apart: 5, of which 5 were waited for; matrix products, arithmetic and copies ran while one was open for 7% of the time, Pallas kernels for 0%

profile of v1, /device:TPU:0, one launch (start us, length us, event | category | flops | bytes accessed | tf_op | source)
XLA Modules:
  0.0 490.7 jit_solution(1182661555488229035)
XLA Ops:
  6.5 0.0 copy-start.1
  6.5 0.0 all-reduce.6.cloned.1.call-start
  6.5 0.8 multiply_convert_fusion.1
  7.3 0.8 div.23
  8.1 1.6 select_reduce_fusion
  9.7 9.2 %fusion.6 = f32[256,32]{1,0:T(8,128)} fusion(bf16[256,8192]{1,0:T(8,128)(2,1)} %param.8, f32[8192]{0:T(1024)S(1)} %div.23, f32[8192]{0:T(1024)S(1)} %get-tuple-element.12, s32[8192]{0:T(1024)} %param.11), kind=kOutput, calls=%fused_computation.11 | convolution fusion | flops 810024960 | bytes 4325376 | tf_op jit(solution)/shard_map/dot_general | solution.py:36
  18.9 9.2 %fusion.7 = f32[256,32]{1,0:T(8,128)} fusion(bf16[256,8192]{1,0:T(8,128)(2,1)} %param.7, f32[8192]{0:T(1024)S(1)} %div.23, f32[8192]{0:T(1024)S(1)} %get-tuple-element.12, s32[8192]{0:T(1024)} %param.11), kind=kOutput, calls=%fused_computation.13 | convolution fusion | flops 810024960 | bytes 4325376 | tf_op jit(solution)/shard_map/dot_general | solution.py:35
  28.1 0.0 all-reduce.6.cloned.1.call-update
  28.2 0.0 all-gather.2.cloned.1.call-start
  28.2 26.4 %all-reduce.6.cloned.1.call-done = (f32[256,32]{1,0:T(8,128)}, f32[32]{0:T(128)}, f32[256,32]{1,0:T(8,128)}) async-done(((f32[256,32]{1,0:T(8,128)}, f32[32]{0:T(128)}, f32[256,32]{1,0:T(8,128)}), (f32[256,32]{1,0:T(8,128)}, f32[32]{0:T(128)}, f32[256,32]{1,0:T(8,128)})) %all-reduce.6.cloned.1.call-update) | async-done | bytes 65680 | tf_op jit(solution)/shard_map/psum | solution.py:38
  54.6 0.7 broadcast_add_fusion
  55.3 0.0 copy-done.1
  55.3 0.0 copy-start.2
  55.3 7.7 %fusion.1 = bf16[256,8192]{1,0:T(8,128)(2,1)} fusion(bf16[256,8192]{1,0:T(8,128)(2,1)} %param.8, f32[8192]{0:T(1024)S(1)} %div.23, s32[8192]{0:T(1024)S(1)} %copy-done.1, f32[256,32]{1,0:T(8,128)} %get-tuple-element.7, f32[32]{0:T(128)S(1)} %broadcast_add_fusion), kind=kOutput, calls=%fused_computation.3 | convolution fusion | flops 816070656 | bytes 8487040 | tf_op jit(solution)/shard_map/dot_general | solution.py:42
  63.0 0.0 all-gather.2.cloned.1.call-update
  63.0 0.2 all-reduce.4.cloned.1.call-start
  63.2 0.0 copy-done.2
  63.2 7.9 %fusion.5 = bf16[1,256,8192]{2,1,0:T(8,128)(2,1)} fusion(bf16[256,8192]{1,0:T(8,128)(2,1)} %param.7, f32[8192]{0:T(1024)S(1)} %get-tuple-element.13, f32[8192]{0:T(1024)S(1)} %div.23, s32[8192]{0:T(1024)S(1)} %copy-done.1, f32[256,32]{1,0:T(8,128)S(1)} %copy-done.2, f32[32]{0:T(128)S(1)} %broadcast_add_fusion), kind=kOutput, calls=%fused_computation.8 | convolution fusion | flops 818167808 | bytes 8519808 | tf_op jit(solution)/shard_map/dot_general | solution.py:41
  71.1 0.0 collective-permute-start
  71.1 7.5 %collective-permute-done = bf16[1,256,8192]{2,1,0:T(8,128)(2,1)} collective-permute-done((bf16[1,256,8192]{2,1,0:T(8,128)(2,1)}, bf16[1,256,8192]{2,1,0:T(8,128)(2,1)}, u32[]{:S(2)}, u32[]{:S(2)}) %collective-permute-start) | collective-permute-done | bytes 4194336 | tf_op jit(solution)/shard_map/ppermute | solution.py:20
  78.6 6.4 %broadcast_select_fusion.3 = (bf16[1,256,8192]{2,1,0:T(8,128)(2,1)S(1)}, bf16[1,256,8192]{2,1,0:T(8,128)(2,1)}) fusion(bf16[1,256,8192]{2,1,0:T(8,128)(2,1)} %fusion.5, bf16[1,256,8192]{2,1,0:T(8,128)(2,1)} %collective-permute-done, pred[]{:T(512)S(6)} %eq.20), kind=kLoop, calls=%fused_computation.19 | loop fusion | flops 4194304 | bytes 16777216 | tf_op jit(solution)/shard_map/jit(_where)/select_n | solution.py:22
  85.0 0.0 copy-start
  85.0 7.7 %pad_maximum_fusion.1 = bf16[2,256,8192]{2,1,0:T(8,128)(2,1)} fusion(bf16[1,256,8192]{2,1,0:T(8,128)(2,1)} %get-tuple-element.11, bf16[1,256,8192]{2,1,0:T(8,128)(2,1)S(1)} %get-tuple-element.10), kind=kLoop, calls=%fused_computation.9 | loop fusion | flops 4194304 | bytes 16777216 | tf_op jit(solution)/shard_map/concatenate | solution.py:22
  92.7 0.0 copy-done
  92.7 1.5 collective-permute-start.1
  94.2 181.3 %collective-permute-done.1 = bf16[2,256,8192]{2,1,0:T(8,128)(2,1)} collective-permute-done((bf16[2,256,8192]{2,1,0:T(8,128)(2,1)}, bf16[2,256,8192]{2,1,0:T(8,128)(2,1)}, u32[]{:S(2)}, u32[]{:S(2)}) %collective-permute-start.1) | collective-permute-done | bytes 8388640 | tf_op jit(solution)/shard_map/ppermute | solution.py:20
  275.5 6.3 %broadcast_select_fusion.1 = (bf16[2,256,8192]{2,1,0:T(8,128)(2,1)S(1)}, bf16[2,256,8192]{2,1,0:T(8,128)(2,1)S(1)}) fusion(bf16[2,256,8192]{2,1,0:T(8,128)(2,1)} %collective-permute-done.1, pred[]{:T(512)S(6)} %eq.19, bf16[1,256,8192]{2,1,0:T(8,128)(2,1)} %get-tuple-element.11, bf16[1,256,8192]{2,1,0:T(8,128)(2,1)} %copy-done), kind=kLoop, calls=%fused_computation.15 | loop fusion | flops 12582912 | bytes 33554432 | tf_op jit(solution)/shard_map/jit(_where)/select_n | solution.py:22
  281.9 6.6 %pad_maximum_fusion = bf16[4,256,8192]{2,1,0:T(8,128)(2,1)} fusion(bf16[2,256,8192]{2,1,0:T(8,128)(2,1)S(1)} %get-tuple-element.9, bf16[2,256,8192]{2,1,0:T(8,128)(2,1)S(1)} %get-tuple-element.8), kind=kLoop, calls=%fused_computation | loop fusion | flops 8388608 | bytes 33554432 | tf_op jit(solution)/shard_map/concatenate | solution.py:22
  288.4 61.7 %all-gather.2.cloned.1.call-done = bf16[1024,8192]{1,0:T(8,128)(2,1)} async-done(((bf16[256,8192]{1,0:T(8,128)(2,1)}), bf16[1024,8192]{1,0:T(8,128)(2,1)}) %all-gather.2.cloned.1.call-update) | async-done | bytes 16777232 | tf_op jit(solution)/shard_map/all_gather | solution.py:48
  350.1 24.3 %convolution_multiply_fusion = f32[1024,1024]{0,1:T(8,128)} fusion(bf16[1024,8192]{1,0:T(8,128)(2,1)} %bitcast.7, bf16[1024,8192]{1,0:T(8,128)(2,1)} %all-gather.2.cloned.1.call-done), kind=kOutput, calls=%fused_computation.20 | convolution fusion | flops 17180917760 | bytes 37748736 | tf_op jit(solution)/shard_map/dot_general | solution.py:46
  374.4 0.0 all-reduce.4.cloned.1.call-update
  374.5 106.2 %all-reduce.4.cloned.1.call-done = f32[1024,4,256]{0,2,1:T(8,128)} async-done(((f32[1024,4,256]{0,2,1:T(8,128)}), f32[1024,4,256]{0,2,1:T(8,128)}) %all-reduce.4.cloned.1.call-update) | async-done | bytes 4194320 | tf_op jit(solution)/shard_map/psum | solution.py:55
  480.7 1.7 constant_dynamic-slice_fusion
  482.4 1.8 copy.9
Async XLA Ops:
  6.5 48.7 %copy-start.1 = (s32[8192]{0:T(1024)S(1)}, s32[8192]{0:T(1024)}, u32[]{:S(2)}) copy-start(s32[8192]{0:T(1024)} %param.11) | copy-start | bytes 98308
  6.5 48.0 %all-reduce.6.cloned.1.call-start = ((), (), s32[]{:S(2)}) async-start(), calls=%async_computation.2 | async-start | bytes 525312 | tf_op jit(solution)/shard_map/psum | solution.py:38
  28.2 322.0 %all-gather.2.cloned.1.call-start = ((), (), s32[]{:S(2)}) async-start(), calls=%async_computation | async-start | bytes 20971520 | tf_op jit(solution)/shard_map/all_gather | solution.py:48
  55.3 7.9 %copy-start.2 = (f32[256,32]{1,0:T(8,128)S(1)}, f32[256,32]{1,0:T(8,128)}, u32[]{:S(2)}) copy-start(f32[256,32]{1,0:T(8,128)} %get-tuple-element.5) | copy-start | bytes 98308
  63.0 417.7 %all-reduce.4.cloned.1.call-start = ((), (), s32[]{:S(2)}) async-start(), calls=%async_computation.1 | async-start | bytes 8388608 | tf_op jit(solution)/shard_map/psum | solution.py:55
  71.1 7.5 %collective-permute-start = (bf16[1,256,8192]{2,1,0:T(8,128)(2,1)}, bf16[1,256,8192]{2,1,0:T(8,128)(2,1)}, u32[]{:S(2)}, u32[]{:S(2)}) collective-permute-start(bf16[1,256,8192]{2,1,0:T(8,128)(2,1)} %fusion.5), channel_id=1, source_target_pairs={{0,2},{2,0},{4,6},{6,4},{1,3},{3,1},{5,7},{7,5},{8,10},{10,8},{12,... | collective-permute-start | bytes 12582920 | tf_op jit(solution)/shard_map/ppermute | solution.py:20
  85.0 7.7 %copy-start = (bf16[1,256,8192]{2,1,0:T(8,128)(2,1)}, bf16[1,256,8192]{2,1,0:T(8,128)(2,1)S(1)}, u32[]{:S(2)}) copy-start(bf16[1,256,8192]{2,1,0:T(8,128)(2,1)S(1)} %get-tuple-element.10) | copy-start | bytes 12582916
  92.7 182.8 %collective-permute-start.1 = (bf16[2,256,8192]{2,1,0:T(8,128)(2,1)}, bf16[2,256,8192]{2,1,0:T(8,128)(2,1)}, u32[]{:S(2)}, u32[]{:S(2)}) collective-permute-start(bf16[2,256,8192]{2,1,0:T(8,128)(2,1)} %pad_maximum_fusion.1), channel_id=1, source_target_pairs={{0,4},{2,6},{4,0},{6,2},{1,5},{3,7},{5,1},{7,3},{8,12},{10,14},{12... | collective-permute-start | bytes 25165832 | tf_op jit(solution)/shard_map/ppermute | solution.py:20
Sparse Core Ops, SparseCore 0:
  28.3 26.2 all-reduce.5
  63.1 286.9 all-gather.1
  374.6 106.0 all-reduce.3
